TPU v7x, 32 devices: a whole 2x2x4 slice. The times are simulated.
32 devices in a mesh: blk: 8 (over z, y), corpus: 4 (over x, core).
Axes of the slice: x: 2, y: 2, z: 4, core: 2. Of those that a mesh axis runs over, the one named last changes fastest.
Arguments:
- queries: bfloat16 [1024, 4096], P('blk', 'corpus'), may hold values from -12 to 12
- passages: bfloat16 [1024, 4096], P('blk', 'corpus'), may hold values from -4 to 4
- table: bfloat16 [1024, 4096], P('corpus'), may hold values from -4 to 4
- neg_owner: int32 [1024, 7], P('blk'), may hold values from 0 to 3, as said below
- neg_row: int32 [1024, 7], P('blk'), may hold values from 0 to 255
- positive: int32 [1024], P('blk'), may hold values from 0 to 1023, each once
- loss_weight: float32 [1024], P('blk'), may hold values from 32 to 256
Outputs:
- losses: float32 [1024], P(('blk', 'corpus'))
- query_grad: float32 [1024, 4096], P('blk', 'corpus')
- passage_grad: float32 [1024, 4096], P('blk', 'corpus')
- table_grad: float32 [1024, 4096], P('corpus', 'blk')
Inputs may be any that keep to these rules, and one draw needn't show every extreme that they name: `neg_owner`: among the 896 references of the queries of one index of blk (aligned blocks of 128 queries), one shard is named exactly 448 times and no shard more often.
All inputs are finite; a program needn't handle non-finite values.
Results may differ from a plain program's by a relative error of at most 0.0065.
Values may be sent and summed in bfloat16 or wider, within the bound.
No kernel may reach another device: no remote copies, remote signals or barrier semaphores. Data moves between devices by JAX's collectives and lax.ppermute only.
A program may use at most 128 MiB of HBM per device.

v0:
```python
import jax
import jax.numpy as jnp
from jax import lax
from jax.sharding import PartitionSpec as P


def hi_lo(mixing):
    upper = mixing.astype(jnp.bfloat16)
    lower = (mixing - upper.astype(jnp.float32)).astype(jnp.bfloat16)
    return (upper, lower)


def per_device(queries, passages, table, neg_owner, neg_row, positive, loss_weight):
    q_rows, col_width = queries.shape
    owner_count = lax.axis_size("corpus")
    blk_count = lax.axis_size("blk")
    factor = (col_width * owner_count) ** (-0.5)
    rows_shard = table.shape[0]
    table_rows = owner_count * rows_shard
    owner_index = lax.axis_index("corpus")
    blk_index = lax.axis_index("blk")
    table_cols = lax.all_to_all(table, "corpus", split_axis=1, concat_axis=0, tiled=True)
    all_passages = lax.all_gather(passages, "blk", axis=0, tiled=True)
    all_queries = lax.all_gather(queries, "blk", axis=0, tiled=True)
    ids = neg_owner * rows_shard + neg_row
    all_ids = lax.all_gather(ids, "blk", axis=0, tiled=True)
    all_rows = all_passages.shape[0]
    logits = lax.dot_general(
        queries, all_passages, (((1,), (1,)), ((), ())), preferred_element_type=jnp.float32
    )
    table_scores = lax.dot_general(
        queries, table_cols, (((1,), (1,)), ((), ())), preferred_element_type=jnp.float32
    )
    row_iota = jnp.arange(table_rows, dtype=jnp.int32)
    picks = ids[:, :, None] == row_iota[None, None, :]
    hard_logits = jnp.sum(jnp.where(picks, table_scores[:, None, :], 0.0), axis=2)
    logits, hard_logits = lax.psum((logits, hard_logits), "corpus")
    logits = logits * factor
    hard_logits = hard_logits * factor
    row_top = jnp.maximum(jnp.max(logits, axis=1), jnp.max(hard_logits, axis=1))
    log_total = row_top + jnp.log(
        jnp.sum(jnp.exp(logits - row_top[:, None]), axis=1)
        + jnp.sum(jnp.exp(hard_logits - row_top[:, None]), axis=1)
    )
    one_hot = positive[:, None] == jnp.arange(all_rows, dtype=jnp.int32)[None, :]
    losses = log_total - jnp.sum(jnp.where(one_hot, logits, 0.0), axis=1)
    share = q_rows // owner_count
    loss_share = lax.dynamic_slice_in_dim(losses, owner_index * share, share)
    weighting = (loss_weight * factor)[:, None]
    soft_grad = (
        weighting * (jnp.exp(logits - log_total[:, None]) - one_hot.astype(jnp.float32))
    ).astype(jnp.bfloat16)
    hard_grad = (weighting * jnp.exp(hard_logits - log_total[:, None])).astype(jnp.bfloat16)
    mixing = jnp.sum(jnp.where(picks, hard_grad.astype(jnp.float32)[:, :, None], 0.0), axis=1)
    mix_hi, mix_lo = hi_lo(mixing)
    left = jnp.concatenate([soft_grad, mix_hi, mix_lo], axis=1)
    right = jnp.concatenate([all_passages, table_cols, table_cols], axis=0)
    query_grad = jnp.dot(left, right, preferred_element_type=jnp.float32)
    soft_cols = lax.all_to_all(soft_grad, "blk", split_axis=1, concat_axis=0, tiled=True)
    passage_grad = lax.dot_general(
        soft_cols, all_queries, (((0,), (0,)), ((), ())), preferred_element_type=jnp.float32
    )
    all_hard = lax.all_gather(hard_grad, "blk", axis=0, tiled=True)
    per_col = blk_count // owner_count
    piece_width = col_width // per_col
    shard = blk_index // per_col
    part = blk_index % per_col
    shard_iota = shard * rows_shard + jnp.arange(rows_shard, dtype=jnp.int32)
    shard_picks = all_ids[:, :, None] == shard_iota[None, None, :]
    shard_mix = jnp.sum(
        jnp.where(shard_picks, all_hard.astype(jnp.float32)[:, :, None], 0.0), axis=1
    )
    shard_hi, shard_lo = hi_lo(shard_mix)
    query_part = lax.dynamic_slice_in_dim(all_queries, part * piece_width, piece_width, axis=1)
    dims = (((0,), (0,)), ((), ()))
    piece = lax.dot_general(
        shard_hi, query_part, dims, preferred_element_type=jnp.float32
    ) + lax.dot_general(shard_lo, query_part, dims, preferred_element_type=jnp.float32)
    perm = []
    for b in range(blk_count):
        for c in range(owner_count):
            dest_b = c * per_col + b % per_col
            dest_c = b // per_col
            perm.append((b * owner_count + c, dest_b * owner_count + dest_c))
    table_grad = lax.ppermute(piece, ("blk", "corpus"), perm)
    return (loss_share, query_grad, passage_grad, table_grad)


def solution(mesh):
    placed = (
        P("blk", "corpus"),
        P("blk", "corpus"),
        P("corpus", None),
        P("blk", None),
        P("blk", None),
        P("blk"),
        P("blk"),
    )
    return jax.shard_map(
        per_device,
        mesh=mesh,
        in_specs=placed,
        out_specs=(
            P(("blk", "corpus")),
            P("blk", "corpus"),
            P("blk", "corpus"),
            P("corpus", "blk"),
        ),
        check_vma=False,
    )
```

profile of v0, /device:TPU:2, one launch (start us, length us, event | category | flops | bytes accessed | tf_op | source)
XLA Modules:
  0.0 190.5 jit_solution(2006193391956256831)
XLA Ops:
  7.2 0.0 all-gather.3.cloned.1.call-start
  7.2 0.7 all-gather.3.cloned.1.call-update
  7.9 3.3 %copy.26 = bf16[256,4096]{0,1:T(8,128)(2,1)S(1)} copy(bf16[256,4096]{1,0:T(8,128)(2,1)} %param.9) | data formatting | bytes 4194304 | tf_op args[2]
  11.2 2.5 %copy.27 = bf16[256,4,1024]{2,0,1:T(8,128)(2,1)} copy(bf16[256,4,1024]{0,2,1:T(8,128)(2,1)S(1)} %bitcast.20) | data formatting | bytes 4194304 | tf_op jit(solution)/shard_map/all_to_all | solution.py:22
  13.7 3.7 %all-to-all-start = ((bf16[256,4,1024]{2,0,1:T(8,128)(2,1)}), bf16[256,4,1024]{2,0,1:T(8,128)(2,1)S(1)}, u32[]{:S(2)}, u32[]{:S(2)}) async-start(bf16[256,4,1024]{2,0,1:T(8,128)(2,1)} %copy.27), calls=%async_computation | async-start | bytes 4194304 | tf_op jit(solution)/shard_map/all_to_all | solution.py:22
  17.4 0.0 copy-start.8
  17.4 0.0 copy-start.9
  17.5 0.0 copy-start.10
  17.5 0.0 copy-start.3
  17.5 0.0 all-reduce.2.cloned.1.call-start
  17.5 42.9 %all-gather.3.cloned.1.call-done = bf16[1024,1024]{1,0:T(8,128)(2,1)} async-done(((bf16[128,1024]{1,0:T(8,128)(2,1)}), bf16[1024,1024]{1,0:T(8,128)(2,1)}) %all-gather.3.cloned.1.call-update) | async-done | bytes 2097168 | tf_op jit(solution)/shard_map/all_gather | solution.py:23
  60.5 0.0 copy-done.2
  60.5 3.2 %fusion.21 = f32[128,1024]{1,0:T(8,128)} fusion(bf16[128,1024]{1,0:T(8,128)(2,1)S(1)} %copy-done.2, bf16[1024,1024]{1,0:T(8,128)(2,1)} %all-gather.3.cloned.1.call-done), kind=kOutput, calls=%fused_computation.41 | convolution fusion | flops 268435456 | bytes 2883584 | tf_op jit(solution)/shard_map/dot_general | solution.py:28
  63.7 0.0 all-reduce.2.cloned.1.call-update
  63.7 0.0 all-gather.5.cloned.1.call-start
  63.7 0.7 all-gather.5.cloned.1.call-update
  64.4 0.0 copy-start.7
  64.5 0.0 copy-done.8
  64.5 0.0 copy-done.9
  64.5 30.6 %all_gather.14 = s32[1024,7]{0,1:T(8,128)S(1)} all-gather(s32[128,7]{0,1:T(8,128)S(1)} %multiply_add_fusion), channel_id=1, replica_groups=mesh['blk'=8,'corpus'=4] {'blk'}, dimensions={0}, use_global_device_ids=true | all-gather | bytes 32256 | tf_op jit(solution)/shard_map/all_gather | solution.py:26
  95.1 0.0 copy-done.10
  95.1 0.0 all-to-all-done
  95.1 0.0 copy-done.3
  95.1 0.8 fusion.22
  96.0 0.6 select_reduce_fusion.2
  96.6 5.9 %psum.15 = f32[128,7]{0,1:T(8,128)S(1)} all-reduce(f32[128,7]{0,1:T(8,128)S(1)} %select_reduce_fusion.2), channel_id=1, replica_groups=mesh['blk'=8,'corpus'=4] {'corpus'}, use_global_device_ids=true, to_apply=%region_3.4 | all-reduce | flops 896 | bytes 7168 | tf_op jit(solution)/shard_map/psum | solution.py:37
  102.5 0.0 all-reduce.2.cloned.1.call-done
  102.5 1.2 multiply_reduce_fusion
  103.7 0.0 copy-done.7
  103.7 1.4 select_reduce_fusion.3
  105.1 2.1 %copy_bitcast_fusion = bf16[128,8,128]{2,0,1:T(8,128)(2,1)} fusion(s32[128]{0:T(128)S(1)} %copy-done.7, f32[128]{0:T(128)S(1)} %get-tuple-element.11, f32[128,1024]{1,0:T(8,128)} %all-reduce.2.cloned.1.call-done, f32[128]{0:T(128)S(1)} %broadcast_multiply_fusion), kind=kLoop, calls=%fused_computation.26 | loop fusion | flops 917504 | bytes 787968 | tf_op jit(solution)/shard_map/all_to_all | solution.py:59
  107.2 3.4 %all-to-all-start.1 = ((bf16[128,8,128]{2,0,1:T(8,128)(2,1)}), bf16[128,8,128]{2,0,1:T(8,128)(2,1)S(1)}, u32[]{:S(2)}, u32[]{:S(2)}) async-start(bf16[128,8,128]{2,0,1:T(8,128)(2,1)} %copy_bitcast_fusion), calls=%async_computation.1 | async-start | bytes 524288 | tf_op jit(solution)/shard_map/all_to_all | solution.py:59
  110.6 33.2 %all_gather.15 = bf16[1024,7]{0,1:T(8,128)(2,1)S(1)} all-gather(bf16[128,7]{0,1:T(8,128)(2,1)S(1)} %get-tuple-element.9), channel_id=1, replica_groups=mesh['blk'=8,'corpus'=4] {'blk'}, dimensions={0}, use_global_device_ids=true | all-gather | bytes 16128 | tf_op jit(solution)/shard_map/all_gather | solution.py:63
  143.8 0.5 select_reduce_fusion.1
  144.3 0.9 subtract_convert_fusion.2
  145.2 2.5 %select_reduce_fusion = f32[1024,256]{1,0:T(8,128)S(1)} fusion(f32[1024,7]{0,1:T(8,128)S(1)} %convert_element_type.40, s32[256]{0:T(256)S(1)} %iota_add_fusion, s32[1024,7]{0,1:T(8,128)S(1)} %all_gather.14), kind=kLoop, calls=%fused_computation | loop fusion | flops 5242880 | bytes 1106944 | tf_op jit(solution)/shard_map/reduce_sum | solution.py:70
  147.7 3.9 %all-gather.5.cloned.1.call-done = bf16[1024,1024]{1,0:T(8,128)(2,1)} async-done(((bf16[128,1024]{1,0:T(8,128)(2,1)}), bf16[1024,1024]{1,0:T(8,128)(2,1)}) %all-gather.5.cloned.1.call-update) | async-done | bytes 2097168 | tf_op jit(solution)/shard_map/all_gather | solution.py:24
  151.7 1.8 fusion.7
  153.5 0.1 copy-done
  153.6 1.3 convolution_add_fusion
  154.9 3.7 %collective-permute-start = (f32[256,512]{1,0:T(8,128)}, f32[256,512]{1,0:T(8,128)S(1)}, u32[]{:S(2)}, u32[]{:S(2)}) collective-permute-start(f32[256,512]{1,0:T(8,128)} %convolution_add_fusion), channel_id=1, source_target_pairs={{0,0},{1,8},{2,16},{3,24},{4,4},{5,12},{6,20},{7,28},{8,1},{9,9},{... | collective-permute-start | bytes 1572872 | tf_op jit(solution)/shard_map/ppermute | solution.py:85
  158.7 0.3 multiply_convert_fusion
  159.0 1.8 fusion
  160.8 0.6 dynamic_slice.6
  161.4 0.0 all-to-all-done.1
  161.4 2.9 %fusion.23 = f32[128,1024]{1,0:T(8,128)} fusion(bf16[1024,128]{1,0:T(8,128)(2,1)S(1)} %bitcast.21, bf16[1024,1024]{1,0:T(8,128)(2,1)} %all-gather.5.cloned.1.call-done), kind=kOutput, calls=%fused_computation.43 | convolution fusion | flops 268435456 | bytes 2883584 | tf_op jit(solution)/shard_map/dot_general | solution.py:60
  164.2 19.0 %collective-permute-done = f32[256,512]{1,0:T(8,128)S(1)} collective-permute-done((f32[256,512]{1,0:T(8,128)}, f32[256,512]{1,0:T(8,128)S(1)}, u32[]{:S(2)}, u32[]{:S(2)}) %collective-permute-start) | collective-permute-done | bytes 524320 | tf_op jit(solution)/shard_map/ppermute | solution.py:85
  183.2 0.8 copy.33
  (19 shorter events, 0.1 us)
Async XLA Ops:
  7.2 53.3 %all-gather.3.cloned.1.call-start = ((), (), s32[]{:S(2)}) async-start(), calls=%async_computation.2 | async-start | bytes 2359296 | tf_op jit(solution)/shard_map/all_gather | solution.py:23
  13.7 46.8 %copy-start.2 = (bf16[128,1024]{1,0:T(8,128)(2,1)S(1)}, bf16[128,1024]{1,0:T(8,128)(2,1)}, u32[]{:S(2)}) copy-start(bf16[128,1024]{1,0:T(8,128)(2,1)} %param.7) | copy-start | bytes 786436
  13.7 81.4 %all-to-all-start = ((bf16[256,4,1024]{2,0,1:T(8,128)(2,1)}), bf16[256,4,1024]{2,0,1:T(8,128)(2,1)S(1)}, u32[]{:S(2)}, u32[]{:S(2)}) async-start(bf16[256,4,1024]{2,0,1:T(8,128)(2,1)} %copy.27), calls=%async_computation | async-start | bytes 4194304 | tf_op jit(solution)/shard_map/all_to_all | solution.py:22
  17.4 47.0 %copy-start.8 = (s32[128,7]{0,1:T(8,128)S(1)}, s32[128,7]{0,1:T(8,128)}, u32[]{:S(2)}) copy-start(s32[128,7]{0,1:T(8,128)} %param.11) | copy-start | bytes 10756
  17.4 47.0 %copy-start.9 = (s32[128,7]{0,1:T(8,128)S(1)}, s32[128,7]{0,1:T(8,128)}, u32[]{:S(2)}) copy-start(s32[128,7]{0,1:T(8,128)} %param.10) | copy-start | bytes 10756
  17.5 77.7 %copy-start.10 = (f32[128]{0:T(128)S(1)}, f32[128]{0:T(128)}, u32[]{:S(2)}) copy-start(f32[128]{0:T(128)} %param.13) | copy-start | bytes 1540
  17.5 77.7 %copy-start.3 = (bf16[128,1024]{1,0:T(8,128)(2,1)S(1)}, bf16[128,1024]{1,0:T(8,128)(2,1)}, u32[]{:S(2)}) copy-start(bf16[128,1024]{1,0:T(8,128)(2,1)} %param.7) | copy-start | bytes 786436
  17.5 85.1 %all-reduce.2.cloned.1.call-start = ((), (), s32[]{:S(2)}) async-start(), calls=%async_computation.3 | async-start | bytes 1048576 | tf_op jit(solution)/shard_map/psum | solution.py:37
  63.7 88.0 %all-gather.5.cloned.1.call-start = ((), (), s32[]{:S(2)}) async-start(), calls=%async_computation.4 | async-start | bytes 2359296 | tf_op jit(solution)/shard_map/all_gather | solution.py:24
  64.4 39.3 %copy-start.7 = (s32[128]{0:T(128)S(1)}, s32[128]{0:T(128)}, u32[]{:S(2)}) copy-start(s32[128]{0:T(128)} %param.12) | copy-start | bytes 1540
  107.2 54.2 %all-to-all-start.1 = ((bf16[128,8,128]{2,0,1:T(8,128)(2,1)}), bf16[128,8,128]{2,0,1:T(8,128)(2,1)S(1)}, u32[]{:S(2)}, u32[]{:S(2)}) async-start(bf16[128,8,128]{2,0,1:T(8,128)(2,1)} %copy_bitcast_fusion), calls=%async_computation.1 | async-start | bytes 524288 | tf_op jit(solution)/shard_map/all_to_all | solution.py:59
  151.7 1.9 %copy-start = (bf16[1024,1024]{1,0:T(8,128)(2,1)S(1)}, bf16[1024,1024]{1,0:T(8,128)(2,1)}, u32[]{:S(2)}) copy-start(bf16[1024,1024]{1,0:T(8,128)(2,1)} %all-gather.5.cloned.1.call-done) | copy-start | bytes 6291460
  153.6 5.0 %copy-start.1 = (f32[128,1024]{1,0:T(8,128)S(1)}, f32[128,1024]{1,0:T(8,128)}, u32[]{:S(2)}) copy-start(f32[128,1024]{1,0:T(8,128)} %all-reduce.2.cloned.1.call-done) | copy-start | bytes 1572868
  153.6 5.3 %copy-start.4 = (bf16[1024,1024]{1,0:T(8,128)(2,1)S(1)}, bf16[1024,1024]{1,0:T(8,128)(2,1)}, u32[]{:S(2)}) copy-start(bf16[1024,1024]{1,0:T(8,128)(2,1)} %all-gather.3.cloned.1.call-done) | copy-start | bytes 6291460
  153.6 5.3 %copy-start.5 = (bf16[128,1024]{1,0:T(8,128)(2,1)S(1)}, bf16[128,1024]{1,0:T(8,128)(2,1)}, u32[]{:S(2)}) copy-start(bf16[128,1024]{1,0:T(8,128)(2,1)} %get-tuple-element.6) | copy-start | bytes 786436
  153.6 5.4 %copy-start.6 = (bf16[128,1024]{1,0:T(8,128)(2,1)S(1)}, bf16[128,1024]{1,0:T(8,128)(2,1)}, u32[]{:S(2)}) copy-start(bf16[128,1024]{1,0:T(8,128)(2,1)} %get-tuple-element.7) | copy-start | bytes 786436
  154.9 28.3 %collective-permute-start = (f32[256,512]{1,0:T(8,128)}, f32[256,512]{1,0:T(8,128)S(1)}, u32[]{:S(2)}, u32[]{:S(2)}) collective-permute-start(f32[256,512]{1,0:T(8,128)} %convolution_add_fusion), channel_id=1, source_target_pairs={{0,0},{1,8},{2,16},{3,24},{4,4},{5,12},{6,20},{7,28},{8,1},{9,9},{... | collective-permute-start | bytes 1572872 | tf_op jit(solution)/shard_map/ppermute | solution.py:85
Sparse Core Ops, SparseCore 0:
  10.1 50.3 all-gather.2
  63.8 30.5 all-reduce.1
  96.6 55.0 all-gather.4
where the time goes:
time: 191 us
  blocking collectives  69.8 us (37%)
  waiting for transfers between devices  67.3 us (35%)
  between operations  14 us (7%)
  matrix products  11.8 us (6%)
  starting transfers between devices  11 us (6%)
  other arithmetic  9.43 us (5%)
  local copies, waits for them, and re-layouts  7.28 us (4%)
    all_gather x1, waiting for transfers between devices, per_device(): all_passages = lax.all_gather(passages, 'blk', axis=0, tiled=True)  42.9 us
    all_gather x1, blocking collectives, per_device(): all_hard = lax.all_gather(hard_grad, 'blk', axis=0, tiled=True)  33.2 us
    all_gather x1, blocking collectives, per_device(): all_ids = lax.all_gather(ids, 'blk', axis=0, tiled=True)  30.6 us
    ppermute x1, waiting for transfers between devices, per_device(): table_grad = lax.ppermute(piece, ('blk', 'corpus'), perm)  19 us
    psum x1, blocking collectives, per_device(): logits, hard_logits = lax.psum((logits, hard_logits), 'corpus')  5.93 us
    unnamed x24, local copies, waits for them, and re-layouts  4.18 us
    all_gather x1, waiting for transfers between devices, per_device(): all_queries = lax.all_gather(queries, 'blk', axis=0, tiled=True)  3.95 us
  transfers between devices with their start and end apart: 6, of which 3 were waited for; matrix products, arithmetic and copies ran while one was open for 14% of the time, Pallas kernels for 0%

commit v1 on v0

--- a/solution.py
+++ b/solution.py
@@ -2,6 +2,13 @@
 import jax.numpy as jnp
 from jax import lax
 from jax.sharding import PartitionSpec as P
+
+
+def _register_node(xin, in_dim):
+    state_now = list(xin.shape[1:])
+    state_now[in_dim] *= xin.shape[0]
+    b_next = jnp.moveaxis(xin, 0, in_dim).reshape(state_now)
+    return b_next
 
 
 def hi_lo(mixing):
@@ -21,7 +28,21 @@
     blk_index = lax.axis_index("blk")
     table_cols = lax.all_to_all(table, "corpus", split_axis=1, concat_axis=0, tiled=True)
     all_passages = lax.all_gather(passages, "blk", axis=0, tiled=True)
-    all_queries = lax.all_gather(queries, "blk", axis=0, tiled=True)
+
+    def form_the_shapes(frame_in, comm_axis, pos_dim):
+        sides = lax.axis_size(comm_axis)
+        pile = [(to_i, (to_i + 1) % sides) for to_i in range(sides)]
+        steps_seen = [frame_in]
+        while len(steps_seen) < sides:
+            finding = lax.ppermute(steps_seen[-1], axis_name=comm_axis, perm=pile)
+            steps_seen.append(finding)
+        v1 = lax.axis_index(comm_axis)
+        n_now = jnp.stack(steps_seen, 0)
+        steps_seen = n_now[(v1 - jnp.arange(sides)) % sides]
+        f_next = _register_node(steps_seen, pos_dim)
+        return f_next
+
+    all_queries = form_the_shapes(queries, "blk", 0)
     ids = neg_owner * rows_shard + neg_row
     all_ids = lax.all_gather(ids, "blk", axis=0, tiled=True)
     all_rows = all_passages.shape[0]

time: 191 us -> 229 us (1.20)
  waiting for transfers between devices: 67.3 us -> 92.1 us
  local copies, waits for them, and re-layouts: 7.28 us -> 16.1 us
  starting transfers between devices: 11 us -> 16 us
  blocking collectives: 69.8 us -> 73.9 us
  matrix products: 11.8 us -> 8.85 us
    ppermute x0 -> x7, waiting for transfers between devices: none -> 44.5 us  [form_the_shapes(): finding = lax.ppermute(steps_seen[-1], axis_name=comm_axis, perm=pile)]
    all_gather x1, waiting for transfers between devices: 42.9 us -> 0.01 us  [per_device(): all_passages = lax.all_gather(passages, 'blk', axis=0, tiled=True)]
    psum x1, waiting for transfers between devices: 0.01 us -> 30.5 us  [per_device(): logits, hard_logits = lax.psum((logits, hard_logits), 'corpus')]
    all_gather x1, blocking collectives: 30.6 us -> 40.2 us  [per_device(): all_ids = lax.all_gather(ids, 'blk', axis=0, tiled=True)]
    all_gather x1, blocking collectives: 33.2 us -> 27.9 us  [per_device(): all_hard = lax.all_gather(hard_grad, 'blk', axis=0, tiled=True)]
    unnamed x24 -> x29, local copies, waits for them, and re-layouts: 4.18 us -> 9.18 us
    all_gather x1 -> x0, waiting for transfers between devices: 3.95 us -> none  [per_device(): all_queries = lax.all_gather(queries, 'blk', axis=0, tiled=True)]
    ppermute x0 -> x7, starting transfers between devices: none -> 3.15 us  [form_the_shapes(): finding = lax.ppermute(steps_seen[-1], axis_name=comm_axis, perm=pile)]
  transfers between devices with their start and end apart: 6 -> 12, of which waited for: 3 -> 6; matrix products, arithmetic and copies ran while one was open for 14% -> 12% of each run, Pallas kernels for 0% -> 0%
where the time goes in v1:
time: 229 us
  waiting for transfers between devices  92.1 us (40%)
  blocking collectives  73.9 us (32%)
  local copies, waits for them, and re-layouts  16.1 us (7%)
  starting transfers between devices  16 us (7%)
  between operations  14.2 us (6%)
  matrix products  8.85 us (4%)
  other arithmetic  7.38 us (3%)
    ppermute x7, waiting for transfers between devices, form_the_shapes(): finding = lax.ppermute(steps_seen[-1], axis_name=comm_axis, perm=pile)  44.5 us
    all_gather x1, blocking collectives, per_device(): all_ids = lax.all_gather(ids, 'blk', axis=0, tiled=True)  40.2 us
    psum x1, waiting for transfers between devices, per_device(): logits, hard_logits = lax.psum((logits, hard_logits), 'corpus')  30.5 us
    all_gather x1, blocking collectives, per_device(): all_hard = lax.all_gather(hard_grad, 'blk', axis=0, tiled=True)  27.9 us
    ppermute x1, waiting for transfers between devices, per_device(): table_grad = lax.ppermute(piece, ('blk', 'corpus'), perm)  16.3 us
    unnamed x29, local copies, waits for them, and re-layouts  9.18 us
    all_to_all x1, starting transfers between devices, per_device(): lax.all_to_all(soft_grad, 'blk', split_axis=1, concat_axis=0, tiled=True)  6.06 us
    psum x1, blocking collectives, per_device(): logits, hard_logits = lax.psum((logits, hard_logits), 'corpus')  5.79 us
  transfers between devices with their start and end apart: 12, of which 6 were waited for; matrix products, arithmetic and copies ran while one was open for 12% of the time, Pallas kernels for 0%

profile of v1, /device:TPU:2, one launch (start us, length us, event | category | flops | bytes accessed | tf_op | source)
XLA Modules:
  0.0 228.6 jit_solution(12053792682658917365)
XLA Ops:
  7.2 0.0 all-gather.2.cloned.1.call-start
  7.2 0.7 all-gather.2.cloned.1.call-update
  7.9 1.6 collective-permute-start
  9.5 3.3 %copy.23 = bf16[256,4096]{0,1:T(8,128)(2,1)S(1)} copy(bf16[256,4096]{1,0:T(8,128)(2,1)} %param.9) | data formatting | bytes 4194304 | tf_op args[2]
  12.7 2.5 %copy.24 = bf16[256,4,1024]{2,0,1:T(8,128)(2,1)} copy(bf16[256,4,1024]{0,2,1:T(8,128)(2,1)S(1)} %bitcast.38) | data formatting | bytes 4194304 | tf_op jit(solution)/shard_map/all_to_all | solution.py:29
  15.2 4.3 %all-to-all-start = ((bf16[256,4,1024]{2,0,1:T(8,128)(2,1)}), bf16[256,4,1024]{2,0,1:T(8,128)(2,1)S(1)}, u32[]{:S(2)}, u32[]{:S(2)}) async-start(bf16[256,4,1024]{2,0,1:T(8,128)(2,1)} %copy.24), calls=%async_computation | async-start | bytes 4194304 | tf_op jit(solution)/shard_map/all_to_all | solution.py:29
  19.5 0.0 collective-permute-done
  19.5 1.6 collective-permute-start.1
  21.1 15.4 %collective-permute-done.1 = bf16[128,1024]{1,0:T(8,128)(2,1)S(1)} collective-permute-done((bf16[128,1024]{1,0:T(8,128)(2,1)S(1)}, bf16[128,1024]{1,0:T(8,128)(2,1)S(1)}, u32[]{:S(2)}, u32[]{:S(2)}) %collective-permute-start.1) | collective-permute-done | bytes 262176 | tf_op jit(solution)/shard_map/ppermute | solution.py:37
  36.6 0.7 bitcast_dynamic-update-slice_fusion.7
  37.3 9.6 %collective-permute-done.2 = bf16[128,1024]{1,0:T(8,128)(2,1)S(1)} collective-permute-done((bf16[128,1024]{1,0:T(8,128)(2,1)S(1)}, bf16[128,1024]{1,0:T(8,128)(2,1)S(1)}, u32[]{:S(2)}, u32[]{:S(2)}) %collective-permute-start.2) | collective-permute-done | bytes 262176 | tf_op jit(solution)/shard_map/ppermute | solution.py:37
  46.9 0.0 collective-permute-start.3
  46.9 40.2 %all_gather.10 = s32[1024,7]{0,1:T(8,128)S(1)} all-gather(s32[128,7]{0,1:T(8,128)S(1)} %multiply_add_fusion), channel_id=1, replica_groups=mesh['blk'=8,'corpus'=4] {'blk'}, dimensions={0}, use_global_device_ids=true | all-gather | bytes 32256 | tf_op jit(solution)/shard_map/all_gather | solution.py:47
  87.1 0.7 bitcast_dynamic-update-slice_fusion.6
  87.8 0.7 bitcast_dynamic-update-slice_fusion.5
  88.5 0.7 bitcast_dynamic-update-slice_fusion.4
  89.2 10.2 %collective-permute-done.4 = bf16[128,1024]{1,0:T(8,128)(2,1)S(1)} collective-permute-done((bf16[128,1024]{1,0:T(8,128)(2,1)S(1)}, bf16[128,1024]{1,0:T(8,128)(2,1)S(1)}, u32[]{:S(2)}, u32[]{:S(2)}) %collective-permute-start.4) | collective-permute-done | bytes 262176 | tf_op jit(solution)/shard_map/ppermute | solution.py:37
  99.5 0.0 collective-permute-start.5
  99.5 0.7 bitcast_dynamic-update-slice_fusion.3
  100.2 0.8 bitcast_dynamic-update-slice_fusion.2
  100.9 9.3 %collective-permute-done.5 = bf16[128,1024]{1,0:T(8,128)(2,1)S(1)} collective-permute-done((bf16[128,1024]{1,0:T(8,128)(2,1)S(1)}, bf16[128,1024]{1,0:T(8,128)(2,1)S(1)}, u32[]{:S(2)}, u32[]{:S(2)}) %collective-permute-start.5) | collective-permute-done | bytes 262176 | tf_op jit(solution)/shard_map/ppermute | solution.py:37
  110.3 0.8 fusion.25
  111.1 0.6 select_reduce_fusion.2
  111.7 5.8 %psum.15 = f32[128,7]{0,1:T(8,128)S(1)} all-reduce(f32[128,7]{0,1:T(8,128)S(1)} %select_reduce_fusion.2), channel_id=1, replica_groups=mesh['blk'=8,'corpus'=4] {'corpus'}, use_global_device_ids=true, to_apply=%region_3.4 | all-reduce | flops 896 | bytes 7168 | tf_op jit(solution)/shard_map/psum | solution.py:58
  117.5 0.7 bitcast_dynamic-update-slice_fusion.1
  118.2 3.2 %fusion.24 = f32[128,1024]{1,0:T(8,128)} fusion(bf16[128,1024]{1,0:T(8,128)(2,1)S(1)} %copy-done.3, bf16[1024,1024]{1,0:T(8,128)(2,1)} %all-gather.2.cloned.1.call-done), kind=kOutput, calls=%fused_computation.58 | convolution fusion | flops 268435456 | bytes 2883584 | tf_op jit(solution)/shard_map/dot_general | solution.py:49
  121.4 0.0 all-reduce.2.cloned.1.call-update
  121.5 0.7 bitcast_dynamic-update-slice_fusion
  122.2 2.3 gather_fusion
  124.5 30.5 %all-reduce.2.cloned.1.call-done = f32[128,1024]{1,0:T(8,128)} async-done(((f32[128,1024]{1,0:T(8,128)}), f32[128,1024]{1,0:T(8,128)}) %all-reduce.2.cloned.1.call-update) | async-done | bytes 524304 | tf_op jit(solution)/shard_map/psum | solution.py:58
  155.1 1.2 multiply_reduce_fusion
  156.3 1.4 select_reduce_fusion.3
  157.7 0.5 select_reduce_fusion.1
  158.2 0.8 subtract_convert_fusion.2
  159.0 0.3 multiply_convert_fusion
  159.3 0.8 copy.26
  160.1 6.1 %all-to-all-start.1 = ((bf16[128,8,128]{0,2,1:T(8,128)(2,1)}), bf16[128,8,128]{0,2,1:T(8,128)(2,1)S(1)}, u32[]{:S(2)}, u32[]{:S(2)}) async-start(bf16[128,8,128]{0,2,1:T(8,128)(2,1)} %bitcast.4), calls=%async_computation.1 | async-start | bytes 524288 | tf_op jit(solution)/shard_map/all_to_all | solution.py:80
  166.2 27.9 %all_gather.11 = bf16[1024,7]{0,1:T(8,128)(2,1)S(1)} all-gather(bf16[128,7]{0,1:T(8,128)(2,1)S(1)} %get-tuple-element.9), channel_id=1, replica_groups=mesh['blk'=8,'corpus'=4] {'blk'}, dimensions={0}, use_global_device_ids=true | all-gather | bytes 16128 | tf_op jit(solution)/shard_map/all_gather | solution.py:84
  194.1 2.5 %select_reduce_fusion = f32[1024,256]{1,0:T(8,128)S(1)} fusion(f32[1024,7]{0,1:T(8,128)S(1)} %convert_element_type.40, s32[256]{0:T(256)S(1)} %iota_add_fusion, s32[1024,7]{0,1:T(8,128)S(1)} %all_gather.10), kind=kLoop, calls=%fused_computation.1 | loop fusion | flops 5242880 | bytes 1106944 | tf_op jit(solution)/shard_map/reduce_sum | solution.py:91
  196.7 0.5 fusion.7
  197.1 0.0 copy-start.5
  197.1 1.3 convolution_add_fusion
  198.4 2.5 %collective-permute-start.7 = (f32[256,512]{1,0:T(8,128)}, f32[256,512]{1,0:T(8,128)S(1)}, u32[]{:S(2)}, u32[]{:S(2)}) collective-permute-start(f32[256,512]{1,0:T(8,128)} %convolution_add_fusion), channel_id=1, source_target_pairs={{0,0},{1,8},{2,16},{3,24},{4,4},{5,12},{6,20},{7,28},{8,1},{9,9},{... | collective-permute-start | bytes 1572872 | tf_op jit(solution)/shard_map/ppermute | solution.py:106
  201.0 0.6 dynamic_slice.6
  201.6 1.8 fusion
  203.4 1.2 convolution_bitcast_fusion
  204.6 16.3 %collective-permute-done.7 = f32[256,512]{1,0:T(8,128)S(1)} collective-permute-done((f32[256,512]{1,0:T(8,128)}, f32[256,512]{1,0:T(8,128)S(1)}, u32[]{:S(2)}, u32[]{:S(2)}) %collective-permute-start.7) | collective-permute-done | bytes 524320 | tf_op jit(solution)/shard_map/ppermute | solution.py:106
  220.9 0.8 copy.36
  (39 shorter events, 0.2 us)
Async XLA Ops:
  7.2 111.0 %all-gather.2.cloned.1.call-start = ((), (), s32[]{:S(2)}) async-start(), calls=%async_computation.2 | async-start | bytes 2359296 | tf_op jit(solution)/shard_map/all_gather | solution.py:30
  7.9 11.6 %collective-permute-start = (bf16[128,1024]{1,0:T(8,128)(2,1)}, bf16[128,1024]{1,0:T(8,128)(2,1)S(1)}, u32[]{:S(2)}, u32[]{:S(2)}) collective-permute-start(bf16[128,1024]{1,0:T(8,128)(2,1)} %param.7), channel_id=1, source_target_pairs={{0,4},{4,8},{8,12},{12,16},{16,20},{20,24},{24,28},{28,0},{1,5},{5... | collective-permute-start | bytes 786440 | tf_op jit(solution)/shard_map/ppermute | solution.py:37
  15.2 4.3 %copy-start.9 = (f32[128]{0:T(128)S(1)}, f32[128]{0:T(128)}, u32[]{:S(2)}) copy-start(f32[128]{0:T(128)} %param.13) | copy-start | bytes 1540
  15.2 5.9 %copy-start.6 = (s32[128,7]{0,1:T(8,128)S(1)}, s32[128,7]{0,1:T(8,128)}, u32[]{:S(2)}) copy-start(s32[128,7]{0,1:T(8,128)} %param.11) | copy-start | bytes 10756
  15.2 5.9 %copy-start.7 = (s32[128,7]{0,1:T(8,128)S(1)}, s32[128,7]{0,1:T(8,128)}, u32[]{:S(2)}) copy-start(s32[128,7]{0,1:T(8,128)} %param.10) | copy-start | bytes 10756
  15.2 21.4 %copy-start.3 = (bf16[128,1024]{1,0:T(8,128)(2,1)S(1)}, bf16[128,1024]{1,0:T(8,128)(2,1)}, u32[]{:S(2)}) copy-start(bf16[128,1024]{1,0:T(8,128)(2,1)} %param.7) | copy-start | bytes 786436
  15.2 95.0 %all-to-all-start = ((bf16[256,4,1024]{2,0,1:T(8,128)(2,1)}), bf16[256,4,1024]{2,0,1:T(8,128)(2,1)S(1)}, u32[]{:S(2)}, u32[]{:S(2)}) async-start(bf16[256,4,1024]{2,0,1:T(8,128)(2,1)} %copy.24), calls=%async_computation | async-start | bytes 4194304 | tf_op jit(solution)/shard_map/all_to_all | solution.py:29
  19.5 135.6 %all-reduce.2.cloned.1.call-start = ((), (), s32[]{:S(2)}) async-start(), calls=%async_computation.3 | async-start | bytes 1048576 | tf_op jit(solution)/shard_map/psum | solution.py:58
  19.5 17.0 %collective-permute-start.1 = (bf16[128,1024]{1,0:T(8,128)(2,1)S(1)}, bf16[128,1024]{1,0:T(8,128)(2,1)S(1)}, u32[]{:S(2)}, u32[]{:S(2)}) collective-permute-start(bf16[128,1024]{1,0:T(8,128)(2,1)S(1)} %collective-permute-done), channel_id=1, source_target_pairs={{0,4},{4,8},{8,12},{12,16},{16,20},{20,24},{24,28},{28,0},{1,5},{5... | collective-permute-start | bytes 786440 | tf_op jit(solution)/shard_map/ppermute | solution.py:37
  36.6 10.3 %collective-permute-start.2 = (bf16[128,1024]{1,0:T(8,128)(2,1)S(1)}, bf16[128,1024]{1,0:T(8,128)(2,1)S(1)}, u32[]{:S(2)}, u32[]{:S(2)}) collective-permute-start(bf16[128,1024]{1,0:T(8,128)(2,1)S(1)} %collective-permute-done.1), channel_id=1, source_target_pairs={{0,4},{4,8},{8,12},{12,16},{16,20},{20,24},{24,28},{28,0},{1,5},{5... | collective-permute-start | bytes 786440 | tf_op jit(solution)/shard_map/ppermute | solution.py:37
  46.9 40.9 %collective-permute-start.3 = (bf16[128,1024]{1,0:T(8,128)(2,1)S(1)}, bf16[128,1024]{1,0:T(8,128)(2,1)S(1)}, u32[]{:S(2)}, u32[]{:S(2)}) collective-permute-start(bf16[128,1024]{1,0:T(8,128)(2,1)S(1)} %collective-permute-done.2), channel_id=1, source_target_pairs={{0,4},{4,8},{8,12},{12,16},{16,20},{20,24},{24,28},{28,0},{1,5},{5... | collective-permute-start | bytes 786440 | tf_op jit(solution)/shard_map/ppermute | solution.py:37
  87.8 11.6 %collective-permute-start.4 = (bf16[128,1024]{1,0:T(8,128)(2,1)S(1)}, bf16[128,1024]{1,0:T(8,128)(2,1)S(1)}, u32[]{:S(2)}, u32[]{:S(2)}) collective-permute-start(bf16[128,1024]{1,0:T(8,128)(2,1)S(1)} %collective-permute-done.3), channel_id=1, source_target_pairs={{0,4},{4,8},{8,12},{12,16},{16,20},{20,24},{24,28},{28,0},{1,5},{5... | collective-permute-start | bytes 786440 | tf_op jit(solution)/shard_map/ppermute | solution.py:37
  99.5 10.8 %collective-permute-start.5 = (bf16[128,1024]{1,0:T(8,128)(2,1)S(1)}, bf16[128,1024]{1,0:T(8,128)(2,1)S(1)}, u32[]{:S(2)}, u32[]{:S(2)}) collective-permute-start(bf16[128,1024]{1,0:T(8,128)(2,1)S(1)} %collective-permute-done.4), channel_id=1, source_target_pairs={{0,4},{4,8},{8,12},{12,16},{16,20},{20,24},{24,28},{28,0},{1,5},{5... | collective-permute-start | bytes 786440 | tf_op jit(solution)/shard_map/ppermute | solution.py:37
  110.2 11.2 %collective-permute-start.6 = (bf16[128,1024]{1,0:T(8,128)(2,1)S(1)}, bf16[128,1024]{1,0:T(8,128)(2,1)S(1)}, u32[]{:S(2)}, u32[]{:S(2)}) collective-permute-start(bf16[128,1024]{1,0:T(8,128)(2,1)S(1)} %collective-permute-done.5), channel_id=1, source_target_pairs={{0,4},{4,8},{8,12},{12,16},{16,20},{20,24},{24,28},{28,0},{1,5},{5... | collective-permute-start | bytes 786440 | tf_op jit(solution)/shard_map/ppermute | solution.py:37
  110.2 11.2 %copy-start = (bf16[256,4,1024]{2,0,1:T(8,128)(2,1)}, bf16[256,4,1024]{2,0,1:T(8,128)(2,1)S(1)}, u32[]{:S(2)}) copy-start(bf16[256,4,1024]{2,0,1:T(8,128)(2,1)S(1)} %all-to-all-done) | copy-start | bytes 6291460
  122.2 34.1 %copy-start.8 = (s32[128]{0:T(128)S(1)}, s32[128]{0:T(128)}, u32[]{:S(2)}) copy-start(s32[128]{0:T(128)} %param.12) | copy-start | bytes 1540
  155.0 3.9 %copy-start.2 = (f32[128,1024]{1,0:T(8,128)S(1)}, f32[128,1024]{1,0:T(8,128)}, u32[]{:S(2)}) copy-start(f32[128,1024]{1,0:T(8,128)} %all-reduce.2.cloned.1.call-done) | copy-start | bytes 1572868
  160.1 43.3 %all-to-all-start.1 = ((bf16[128,8,128]{0,2,1:T(8,128)(2,1)}), bf16[128,8,128]{0,2,1:T(8,128)(2,1)S(1)}, u32[]{:S(2)}, u32[]{:S(2)}) async-start(bf16[128,8,128]{0,2,1:T(8,128)(2,1)} %bitcast.4), calls=%async_computation.1 | async-start | bytes 524288 | tf_op jit(solution)/shard_map/all_to_all | solution.py:80
  196.6 4.9 %copy-start.4 = (bf16[1024,1024]{1,0:T(8,128)(2,1)S(1)}, bf16[1024,1024]{1,0:T(8,128)(2,1)}, u32[]{:S(2)}) copy-start(bf16[1024,1024]{1,0:T(8,128)(2,1)} %all-gather.2.cloned.1.call-done) | copy-start | bytes 6291460
  197.1 4.4 %copy-start.1 = (bf16[256,4,1024]{2,0,1:T(8,128)(2,1)S(1)}, bf16[256,4,1024]{2,0,1:T(8,128)(2,1)}, u32[]{:S(2)}) copy-start(bf16[256,4,1024]{2,0,1:T(8,128)(2,1)} %copy-done) | copy-start | bytes 6291460
  197.1 4.4 %copy-start.5 = (bf16[128,1024]{1,0:T(8,128)(2,1)S(1)}, bf16[128,1024]{1,0:T(8,128)(2,1)}, u32[]{:S(2)}) copy-start(bf16[128,1024]{1,0:T(8,128)(2,1)} %get-tuple-element.7) | copy-start | bytes 786436
  198.4 22.5 %collective-permute-start.7 = (f32[256,512]{1,0:T(8,128)}, f32[256,512]{1,0:T(8,128)S(1)}, u32[]{:S(2)}, u32[]{:S(2)}) collective-permute-start(f32[256,512]{1,0:T(8,128)} %convolution_add_fusion), channel_id=1, source_target_pairs={{0,0},{1,8},{2,16},{3,24},{4,4},{5,12},{6,20},{7,28},{8,1},{9,9},{... | collective-permute-start | bytes 1572872 | tf_op jit(solution)/shard_map/ppermute | solution.py:106
Sparse Core Ops, SparseCore 0:
  10.1 60.8 all-gather.1
  121.6 33.4 all-reduce.1
